TPU v7x, 512 devices: a whole 4x8x8 slice. The times are simulated.
512 devices in a mesh: rep: 32 (over x, z), tp: 16 (over y, core).
Axes of the slice: x: 4, y: 8, z: 8, core: 2. Of those that a mesh axis runs over, the one named last changes fastest.
Arguments:
- queries: bfloat16 [10240, 8192], P('rep', 'tp'), may hold values from -30 to 30
- fresh_kv: bfloat16 [10240, 4096], P('rep', 'tp'), may hold values from -6 to 6, as said below
- kv_cache: bfloat16 [1408, 16, 8, 256], P('rep', 'tp'), may hold values from -6 to 6, as said below
- cached_len: int32 [640], P('rep'), may hold values from 1 to 48, as said below
- page_table: int32 [640, 6], P('rep'), may hold values from 0 to 43, as said below
- out_weight: bfloat16 [8192, 4096], P('tp'), may hold values from -0.09375 to 0.09375
- adapter_down: bfloat16 [64, 64, 8192], P('rep', None, 'tp'), may hold values from -0.0625 to 0.0625
- pooled_up_weight: bfloat16 [64, 64, 4096], P('rep', None, 'tp'), may hold values from -0.75 to 0.75
- adapter_ids: int32 [640], P('rep'), may hold values from 0 to 63, as said below
- pool_slot: int32 [64], replicated, may hold values from 0 to 63, as said below
Outputs:
- adapted_output: bfloat16 [10240, 4096], P('rep', 'tp')
Inputs may be any that keep to these rules, and one draw needn't show every extreme that they name: `kv_cache`: slots that hold the same key-value head are equal. `fresh_kv`: slots that hold the same key-value head are equal. `cached_len`: A row with cached length n uses its first ceil(n / 8) page table entries; in every replica some row has 48. `page_table`: entries index the 44 pages of the row's own replica. The pages that a row uses are distinct, no page is used by two rows of one replica, every page of a replica is used, and entries past a row's used pages repeat its first page. `adapter_ids`: row r of replica i is entry i * 20 + r. The owner of adapter a is replica pool_slot[a] // 2. Within one replica at most 2 rows name adapters of one owner, and one owner, the same for all replicas, is named by exactly 2 rows of every replica. A permutation: adapter a's blocks are adapter_down[pool_slot[a]] and pooled_up_weight[pool_slot[a]].
All inputs are finite; a program needn't handle non-finite values.
Results may differ from a plain program's by a relative error of at most 0.023.
Values may be sent and summed in bfloat16 or wider, within the bound.
No kernel may reach another device: no remote copies, remote signals or barrier semaphores. Data moves between devices by JAX's collectives and lax.ppermute only.
A program may use at most 64 MiB of HBM per device.

v0:
```python
import math
import jax
import jax.numpy as jnp
from jax import lax
from jax.sharding import PartitionSpec as P

ADAPTER_SCALE = 2.0


def shards(
    queries,
    fresh_kv,
    kv_cache,
    cached_len,
    page_table,
    out_weight,
    adapter_down,
    pooled_up_weight,
    adapter_ids,
    pool_slot,
):
    row_count = cached_len.shape[0]
    token_count = queries.shape[0]
    per_row = token_count // row_count
    slot_count = kv_cache.shape[1]
    page_len = kv_cache.shape[2]
    head_dim = kv_cache.shape[3] // 2
    feat_width = queries.shape[1]
    head_count = feat_width // head_dim
    heads_per_slot = head_count // slot_count
    cache_span = page_table.shape[1] * page_len
    output_columns = pooled_up_weight.shape[2]
    rank_size = adapter_down.shape[1]
    paged_kv = (
        kv_cache[page_table]
        .transpose(0, 2, 1, 3, 4)
        .reshape(row_count, slot_count, cache_span, 2 * head_dim)
    )
    recent = fresh_kv.reshape(row_count, per_row, slot_count, 2 * head_dim).transpose(0, 2, 1, 3)
    entries = jnp.concatenate([paged_kv, recent], axis=2)
    key_part = entries[..., :head_dim]
    value_part = entries[..., head_dim:]
    query_rows = queries.reshape(
        row_count, per_row, slot_count, heads_per_slot, head_dim
    ).transpose(0, 2, 1, 3, 4)
    query_rows = query_rows.reshape(row_count, slot_count, per_row * heads_per_slot, head_dim)
    scores = jnp.einsum(
        "rsad,rskd->rsak", query_rows, key_part, preferred_element_type=jnp.float32
    ) / math.sqrt(head_dim)
    entry_ids = jnp.arange(cache_span + per_row)[None, None, None, :]
    token_ids = (jnp.arange(per_row * heads_per_slot) // heads_per_slot)[None, None, :, None]
    allowed = jnp.where(
        entry_ids < cache_span,
        entry_ids < cached_len[:, None, None, None],
        entry_ids - cache_span <= token_ids,
    )
    scores = jnp.where(allowed, scores, -jnp.inf)
    peak_score = jnp.max(scores, axis=-1, keepdims=True)
    raised = jnp.exp(scores - peak_score)
    weights = (raised / jnp.sum(raised, axis=-1, keepdims=True)).astype(jnp.bfloat16)
    attended = jnp.einsum(
        "rsak,rskd->rsad", weights, value_part, preferred_element_type=jnp.float32
    ).astype(jnp.bfloat16)
    attended = attended.reshape(row_count, slot_count, per_row, heads_per_slot, head_dim).transpose(
        0, 2, 1, 3, 4
    )
    attended = attended.reshape(token_count, feat_width)
    plain_output = (
        lax.psum_scatter(
            lax.dot_general(
                out_weight, attended, (((0,), (1,)), ((), ())), preferred_element_type=jnp.float32
            ).astype(jnp.bfloat16),
            "tp",
            scatter_dimension=0,
            tiled=True,
        )
        .astype(jnp.float32)
        .T
    )
    slot_hits = adapter_ids[:, None] == jnp.arange(pool_slot.shape[0])[None, :]
    pool_position = jnp.sum(jnp.where(slot_hits, pool_slot[None, :], 0), axis=1)
    by_row = attended.reshape(row_count, per_row, feat_width)
    replicas = lax.axis_size("rep")
    local_count = adapter_down.shape[0]
    capacity = (row_count + replicas - 1) // replicas + 1
    owner_of = pool_position // local_count
    local_slot = pool_position % local_count
    same_owner = owner_of[:, None] == owner_of[None, :]
    earlier = jnp.arange(row_count)[None, :] < jnp.arange(row_count)[:, None]
    seat_of = jnp.sum(same_owner & earlier, axis=1)
    target = owner_of * capacity + seat_of
    placing = jnp.arange(replicas * capacity)[:, None] == target[None, :]
    placing_mat = placing.astype(jnp.bfloat16)
    wanted = (jnp.sum(jnp.where(placing, local_slot[None, :] + 1, 0), axis=1) - 1).reshape(
        replicas, capacity
    )
    choose = (
        lax.all_to_all(wanted, "rep", split_axis=0, concat_axis=0, tiled=True)[:, :, None]
        == jnp.arange(local_count)[None, None, :]
    ).astype(jnp.bfloat16)
    down_blocks = jnp.einsum(
        "smj,jkf->smkf", choose, adapter_down, preferred_element_type=jnp.float32
    ).astype(jnp.bfloat16)
    up_blocks = jnp.einsum(
        "smj,jkd->smkd", choose, pooled_up_weight, preferred_element_type=jnp.float32
    ).astype(jnp.bfloat16)
    down_got = lax.all_to_all(down_blocks, "rep", split_axis=0, concat_axis=0, tiled=True)
    up_got = lax.all_to_all(up_blocks, "rep", split_axis=0, concat_axis=0, tiled=True)
    down_got = down_got.reshape(replicas * capacity, rank_size, feat_width)
    up_got = up_got.reshape(replicas * capacity, rank_size, output_columns)
    down_sel = jnp.einsum(
        "sr,skf->rkf", placing_mat, down_got, preferred_element_type=jnp.float32
    ).astype(jnp.bfloat16)
    up_sel = jnp.einsum(
        "sr,skd->rkd", placing_mat, up_got, preferred_element_type=jnp.float32
    ).astype(jnp.bfloat16)
    shrink_part = jnp.einsum("rqf,rkf->rqk", by_row, down_sel, preferred_element_type=jnp.float32)
    down_projected = lax.psum(shrink_part.astype(jnp.bfloat16), "tp")
    adapter_correction = jnp.einsum(
        "owe,oet->owt", down_projected, up_sel, preferred_element_type=jnp.float32
    ).astype(jnp.bfloat16)
    adapted_output = plain_output + ADAPTER_SCALE * adapter_correction.reshape(
        token_count, output_columns
    ).astype(jnp.float32)
    return adapted_output.astype(jnp.bfloat16)


def solution(mesh):
    return jax.shard_map(
        shards,
        mesh=mesh,
        in_specs=(
            P("rep", "tp"),
            P("rep", "tp"),
            P("rep", "tp", None, None),
            P("rep"),
            P("rep", None),
            P("tp", None),
            P("rep", None, "tp"),
            P("rep", None, "tp"),
            P("rep"),
            P(),
        ),
        out_specs=P("rep", "tp"),
        check_vma=False,
    )
```

profile of v0, /device:TPU:64, one launch (start us, length us, event | category | flops | bytes accessed | tf_op | source)
XLA Modules:
  0.0 253.9 jit_solution(10275384888598889129)
XLA Ops:
  6.5 0.9 select_reduce_fusion.1
  7.4 0.2 convert_reduce_fusion
  7.6 0.1 select_reduce_fusion
  7.7 0.1 sub.34
  7.8 21.0 %all_to_all.16 = s32[32,1,2]{2,1,0:T(1,128)S(1)} all-to-all(s32[32,1,2]{2,1,0:T(1,128)S(1)} %bitcast.62), channel_id=1, replica_groups=mesh['rep'=32,'tp'=16] {'rep'}, dimensions={0} | all-to-all | bytes 512 | tf_op jit(solution)/shard_map/all_to_all | solution.py:98
  28.9 0.1 copy.38
  29.0 1.6 convolution_convert_fusion.2
  30.6 2.5 copy.44
  33.1 5.2 %all-to-all-start.2 = ((bf16[32,2,64,256]{3,2,1,0:T(8,128)(2,1)}), bf16[32,2,64,256]{3,2,1,0:T(8,128)(2,1)S(1)}, u32[]{:S(2)}, u32[]{:S(2)}) async-start(bf16[32,2,64,256]{3,2,1,0:T(8,128)(2,1)} %copy.44), calls=%async_computation.3 | async-start | bytes 4194304 | tf_op jit(solution)/shard_map/all_to_all | solution.py:108
  38.3 1.3 convolution_convert_fusion.1
  39.6 4.3 %copy.40 = bf16[32,2,64,512]{3,2,1,0:T(8,128)(2,1)} copy(bf16[32,2,64,512]{3,0,2,1:T(8,128)(2,1)S(1)} %convolution_convert_fusion.1) | data formatting | bytes 8388608 | tf_op jit(solution)/shard_map/convert_element_type | solution.py:103
  43.9 43.8 %all-to-all-done.2 = bf16[32,2,64,256]{3,2,1,0:T(8,128)(2,1)S(1)} async-done(((bf16[32,2,64,256]{3,2,1,0:T(8,128)(2,1)}), bf16[32,2,64,256]{3,2,1,0:T(8,128)(2,1)S(1)}, u32[]{:S(2)}, u32[]{:S(2)}) %all-to-all-start.2) | async-done | bytes 2097184 | tf_op jit(solution)/shard_map/all_to_all | solution.py:108
  87.7 5.8 %all-to-all-start.1 = ((bf16[32,2,64,512]{3,2,1,0:T(8,128)(2,1)}), bf16[32,2,64,512]{3,2,1,0:T(8,128)(2,1)}, u32[]{:S(2)}, u32[]{:S(2)}) async-start(bf16[32,2,64,512]{3,2,1,0:T(8,128)(2,1)} %copy.40), calls=%async_computation.2 | async-start | bytes 8388608 | tf_op jit(solution)/shard_map/all_to_all | solution.py:107
  93.5 0.2 reduce-scatter.2.cloned.1.call-start
  93.8 0.1 copy.35
  93.9 0.1 reshape.210
  94.0 0.2 reshape.202
  94.2 0.7 gather_fusion
  95.0 0.1 broadcast_compare_fusion
  95.0 0.4 fusion.56
  95.5 1.2 fusion.17
  96.7 1.7 convolution_convert_fusion.3
  98.4 0.2 reshape_transpose_reshape.4
  98.6 5.4 %fusion.1 = bf16[4096,320]{0,1:T(8,128)(2,1)} fusion(bf16[320,512]{1,0:T(8,128)(2,1)S(1)} %reshape_transpose_reshape.4, bf16[512,4096]{1,0:T(8,128)(2,1)} %param.15), kind=kOutput, calls=%fused_computation.3 | convolution fusion | flops 1343488000 | bytes 7143424 | tf_op jit(solution)/shard_map/dot_general | solution.py:70
  104.0 0.2 reshape_reshape_transpose_reshape.3
  104.2 1.3 fusion.9
  105.4 82.9 %all-to-all-done.1 = bf16[32,2,64,512]{3,2,1,0:T(8,128)(2,1)} async-done(((bf16[32,2,64,512]{3,2,1,0:T(8,128)(2,1)}), bf16[32,2,64,512]{3,2,1,0:T(8,128)(2,1)}, u32[]{:S(2)}, u32[]{:S(2)}) %all-to-all-start.1) | async-done | bytes 4194336 | tf_op jit(solution)/shard_map/all_to_all | solution.py:107
  188.4 6.7 %fusion.6 = bf16[20,64,512]{2,0,1:T(8,128)(2,1)S(1)} fusion(bf16[64,64,512]{2,1,0:T(8,128)(2,1)} %bitcast.14, s32[20]{0:T(128)S(1)} %multiply_add_fusion), kind=kOutput, calls=%fused_computation.10 | convolution fusion | flops 84542720 | bytes 5505104 | tf_op jit(solution)/shard_map/sr,skf->rkf/dot_general | solution.py:111
  195.1 0.5 fusion.20
  195.6 49.5 %psum.7 = bf16[20,16,64]{2,1,0:T(8,128)(2,1)S(1)} all-reduce(bf16[20,16,64]{2,1,0:T(8,128)(2,1)S(1)} %fusion.20), channel_id=1, replica_groups=mesh['rep'=32,'tp'=16] {'tp'}, use_global_device_ids=true, to_apply=%region_6.7 | all-reduce | flops 20480 | bytes 81920 | tf_op jit(solution)/shard_map/psum | solution.py:118
  245.1 0.2 fusion.19
  245.4 1.6 fusion.30
  (22 shorter events, 0.2 us)
Async XLA Ops:
  6.5 87.7 %copy-start = (bf16[44,1,8,256]{3,2,1,0:T(8,128)(2,1)S(1)}, bf16[44,1,8,256]{3,2,1,0:T(8,128)(2,1)}, u32[]{:S(2)}) copy-start(bf16[44,1,8,256]{3,2,1,0:T(8,128)(2,1)} %param.12) | copy-start | bytes 540676
  33.1 5.2 %copy-start.2 = (bf16[2,64,512]{2,1,0:T(8,128)(2,1)S(1)}, bf16[2,64,512]{2,1,0:T(8,128)(2,1)}, u32[]{:S(2)}) copy-start(bf16[2,64,512]{2,1,0:T(8,128)(2,1)} %param.16) | copy-start | bytes 393220
  33.1 54.6 %all-to-all-start.2 = ((bf16[32,2,64,256]{3,2,1,0:T(8,128)(2,1)}), bf16[32,2,64,256]{3,2,1,0:T(8,128)(2,1)S(1)}, u32[]{:S(2)}, u32[]{:S(2)}) async-start(bf16[32,2,64,256]{3,2,1,0:T(8,128)(2,1)} %copy.44), calls=%async_computation.3 | async-start | bytes 4194304 | tf_op jit(solution)/shard_map/all_to_all | solution.py:108
  43.9 49.8 %copy-start.3 = (s32[20,6]{0,1:T(8,128)S(1)}, s32[20,6]{0,1:T(8,128)}, u32[]{:S(2)}) copy-start(s32[20,6]{0,1:T(8,128)} %param.14) | copy-start | bytes 1444
  43.9 50.0 %copy-start.1 = (bf16[320,512]{1,0:T(8,128)(2,1)S(1)}, bf16[320,512]{1,0:T(8,128)(2,1)}, u32[]{:S(2)}) copy-start(bf16[320,512]{1,0:T(8,128)(2,1)} %param.10) | copy-start | bytes 983044
  43.9 50.9 %copy-start.4 = (s32[20]{0:T(128)S(1)}, s32[20]{0:T(128)}, u32[]{:S(2)}) copy-start(s32[20]{0:T(128)} %param.13) | copy-start | bytes 244
  43.9 51.1 %copy-start.5 = (bf16[320,256]{1,0:T(8,128)(2,1)S(1)}, bf16[320,256]{1,0:T(8,128)(2,1)}, u32[]{:S(2)}) copy-start(bf16[320,256]{1,0:T(8,128)(2,1)} %param.11) | copy-start | bytes 491524
  87.7 100.6 %all-to-all-start.1 = ((bf16[32,2,64,512]{3,2,1,0:T(8,128)(2,1)}), bf16[32,2,64,512]{3,2,1,0:T(8,128)(2,1)}, u32[]{:S(2)}, u32[]{:S(2)}) async-start(bf16[32,2,64,512]{3,2,1,0:T(8,128)(2,1)} %copy.40), calls=%async_computation.2 | async-start | bytes 8388608 | tf_op jit(solution)/shard_map/all_to_all | solution.py:107
  93.5 151.9 %reduce-scatter.2.cloned.1.call-start = ((), (), s32[]{:S(2)}) async-start(), calls=%async_computation.4 | async-start | bytes 2785280 | tf_op jit(solution)/shard_map/reduce_scatter | solution.py:69
Sparse Core Ops, SparseCore 0:
  104.1 66.3 reduce-scatter.1
where the time goes:
time: 254 us
  waiting for transfers between devices  127 us (50%)
  blocking collectives  70.6 us (28%)
  matrix products  20.3 us (8%)
  between operations  13.6 us (5%)
  starting transfers between devices  11.2 us (4%)
  local copies, waits for them, and re-layouts  8.47 us (3%)
  other arithmetic  2.98 us (1%)
    all_to_all x1, waiting for transfers between devices, shards(): lax.all_to_all(down_blocks, 'rep', split_axis=0, concat_axis=0, tiled=True)  82.9 us
    psum x1, blocking collectives, shards(): down_projected = lax.psum(shrink_part.astype(jnp.bfloat16), 'tp')  49.5 us
    all_to_all x1, waiting for transfers between devices, shards(): lax.all_to_all(up_blocks, 'rep', split_axis=0, concat_axis=0, tiled=True)  43.8 us
    all_to_all x1, blocking collectives, shards(): lax.all_to_all(wanted, 'rep', split_axis=0, concat_axis=0, tiled=True)  21 us
    dot_general x1, matrix products, shards(): jnp.einsum('sr,skf->rkf', placing_mat, down_got, preferred_element_type=j...  6.75 us
    all_to_all x1, starting transfers between devices, shards(): lax.all_to_all(down_blocks, 'rep', split_axis=0, concat_axis=0, tiled=True)  5.76 us
    dot_general x1, matrix products, shards(): lax.dot_general(out_weight, attended, (((0,), (1,)), ((), ())), preferred...  5.37 us
    all_to_all x1, starting transfers between devices, shards(): lax.all_to_all(up_blocks, 'rep', split_axis=0, concat_axis=0, tiled=True)  5.2 us
  transfers between devices with their start and end apart: 3, of which 2 were waited for; matrix products, arithmetic and copies ran while one was open for 10% of the time, Pallas kernels for 0%

commit v1 on v0

--- a/solution.py
+++ b/solution.py
@@ -115,7 +115,11 @@
         "sr,skd->rkd", placing_mat, up_got, preferred_element_type=jnp.float32
     ).astype(jnp.bfloat16)
     shrink_part = jnp.einsum("rqf,rkf->rqk", by_row, down_sel, preferred_element_type=jnp.float32)
-    down_projected = lax.psum(shrink_part.astype(jnp.bfloat16), "tp")
+
+    def state_the_grid(view, axis_tag):
+        return jax.lax.all_gather(view, axis_name=axis_tag).sum(axis=0)
+
+    down_projected = state_the_grid(shrink_part.astype(jnp.bfloat16), "tp")
     adapter_correction = jnp.einsum(
         "owe,oet->owt", down_projected, up_sel, preferred_element_type=jnp.float32
     ).astype(jnp.bfloat16)

time: 254 us -> 230 us (0.906)
  the two profiles are of different devices: /device:TPU:64 before, /device:TPU:1 now
where the time goes in v1:
time: 230 us; the launch traced here: 229 us
  waiting for transfers between devices  128 us (56%)
  blocking collectives  45.7 us (20%)
  matrix products  20.3 us (9%)
  between operations  13.6 us (6%)
  starting transfers between devices  10.6 us (5%)
  local copies, waits for them, and re-layouts  8.47 us (4%)
  other arithmetic  3.25 us (1%)
    all_to_all x1, waiting for transfers between devices, shards(): lax.all_to_all(down_blocks, 'rep', split_axis=0, concat_axis=0, tiled=True)  83.8 us
    all_to_all x1, waiting for transfers between devices, shards(): lax.all_to_all(up_blocks, 'rep', split_axis=0, concat_axis=0, tiled=True)  43.8 us
    all_gather x1, blocking collectives, state_the_grid(): return jax.lax.all_gather(view, axis_name=axis_tag).sum(axis=0)  23.5 us
    all_to_all x1, blocking collectives, shards(): lax.all_to_all(wanted, 'rep', split_axis=0, concat_axis=0, tiled=True)  22.2 us
    dot_general x1, matrix products, shards(): jnp.einsum('sr,skf->rkf', placing_mat, down_got, preferred_element_type=j...  6.75 us
    all_to_all x1, starting transfers between devices, shards(): lax.all_to_all(down_blocks, 'rep', split_axis=0, concat_axis=0, tiled=True)  6.2 us
    dot_general x1, matrix products, shards(): lax.dot_general(out_weight, attended, (((0,), (1,)), ((), ())), preferred...  5.37 us
  transfers between devices with their start and end apart: 3, of which 2 were waited for; matrix products, arithmetic and copies ran while one was open for 11% of the time, Pallas kernels for 0%

profile of v1, /device:TPU:1, one launch (start us, length us, event | category | flops | bytes accessed | tf_op | source)
XLA Modules:
  0.0 229.5 jit_solution(10176671151164792861)
XLA Ops:
  6.5 0.9 select_reduce_fusion.1
  7.4 0.2 convert_reduce_fusion
  7.6 0.1 select_reduce_fusion
  7.7 0.1 sub.34
  7.8 22.2 %all_to_all.16 = s32[32,1,2]{2,1,0:T(1,128)S(1)} all-to-all(s32[32,1,2]{2,1,0:T(1,128)S(1)} %bitcast.64), channel_id=1, replica_groups=mesh['rep'=32,'tp'=16] {'rep'}, dimensions={0} | all-to-all | bytes 512 | tf_op jit(solution)/shard_map/all_to_all | solution.py:98
  30.0 0.1 copy.38
  30.1 1.6 convolution_convert_fusion.2
  31.7 2.5 %copy.44 = bf16[32,2,64,256]{3,2,1,0:T(8,128)(2,1)} copy(bf16[32,2,64,256]{3,0,2,1:T(8,128)(2,1)S(1)} %convolution_convert_fusion.2) | data formatting | bytes 4194304 | tf_op jit(solution)/shard_map/convert_element_type | solution.py:106
  34.2 4.1 %all-to-all-start.2 = ((bf16[32,2,64,256]{3,2,1,0:T(8,128)(2,1)}), bf16[32,2,64,256]{3,2,1,0:T(8,128)(2,1)S(1)}, u32[]{:S(2)}, u32[]{:S(2)}) async-start(bf16[32,2,64,256]{3,2,1,0:T(8,128)(2,1)} %copy.44), calls=%async_computation.3 | async-start | bytes 4194304 | tf_op jit(solution)/shard_map/all_to_all | solution.py:108
  38.4 1.3 convolution_convert_fusion.1
  39.7 4.3 %copy.40 = bf16[32,2,64,512]{3,2,1,0:T(8,128)(2,1)} copy(bf16[32,2,64,512]{3,0,2,1:T(8,128)(2,1)S(1)} %convolution_convert_fusion.1) | data formatting | bytes 8388608 | tf_op jit(solution)/shard_map/convert_element_type | solution.py:103
  44.0 43.8 %all-to-all-done.2 = bf16[32,2,64,256]{3,2,1,0:T(8,128)(2,1)S(1)} async-done(((bf16[32,2,64,256]{3,2,1,0:T(8,128)(2,1)}), bf16[32,2,64,256]{3,2,1,0:T(8,128)(2,1)S(1)}, u32[]{:S(2)}, u32[]{:S(2)}) %all-to-all-start.2) | async-done | bytes 2097184 | tf_op jit(solution)/shard_map/all_to_all | solution.py:108
  87.8 6.2 %all-to-all-start.1 = ((bf16[32,2,64,512]{3,2,1,0:T(8,128)(2,1)}), bf16[32,2,64,512]{3,2,1,0:T(8,128)(2,1)}, u32[]{:S(2)}, u32[]{:S(2)}) async-start(bf16[32,2,64,512]{3,2,1,0:T(8,128)(2,1)} %copy.40), calls=%async_computation.2 | async-start | bytes 8388608 | tf_op jit(solution)/shard_map/all_to_all | solution.py:107
  94.0 0.2 reduce-scatter.2.cloned.1.call-start
  94.3 0.1 copy.35
  94.4 0.1 reshape.210
  94.5 0.2 reshape.202
  94.7 0.7 gather_fusion
  95.6 0.4 fusion.56
  96.0 1.2 fusion.17
  97.2 1.7 convolution_convert_fusion.3
  98.9 0.2 reshape_transpose_reshape.4
  99.1 5.4 %fusion.1 = bf16[4096,320]{0,1:T(8,128)(2,1)} fusion(bf16[320,512]{1,0:T(8,128)(2,1)S(1)} %reshape_transpose_reshape.4, bf16[512,4096]{1,0:T(8,128)(2,1)} %param.15), kind=kOutput, calls=%fused_computation.3 | convolution fusion | flops 1343488000 | bytes 7143424 | tf_op jit(solution)/shard_map/dot_general | solution.py:70
  104.5 0.2 reshape_reshape_transpose_reshape.3
  104.7 1.3 fusion.9
  106.0 83.8 %all-to-all-done.1 = bf16[32,2,64,512]{3,2,1,0:T(8,128)(2,1)} async-done(((bf16[32,2,64,512]{3,2,1,0:T(8,128)(2,1)}), bf16[32,2,64,512]{3,2,1,0:T(8,128)(2,1)}, u32[]{:S(2)}, u32[]{:S(2)}) %all-to-all-start.1) | async-done | bytes 4194336 | tf_op jit(solution)/shard_map/all_to_all | solution.py:107
  189.7 6.7 %fusion.6 = bf16[20,64,512]{2,0,1:T(8,128)(2,1)S(1)} fusion(bf16[64,64,512]{2,1,0:T(8,128)(2,1)} %bitcast.14, s32[20]{0:T(128)S(1)} %multiply_add_fusion), kind=kOutput, calls=%fused_computation.10 | convolution fusion | flops 84542720 | bytes 5505104 | tf_op jit(solution)/shard_map/sr,skf->rkf/dot_general | solution.py:111
  196.5 0.5 fusion.20
  197.0 23.5 %all-gather = bf16[320,16,64]{2,1,0:T(8,128)(2,1)S(1)} all-gather(bf16[20,16,64]{2,1,0:T(8,128)(2,1)S(1)} %fusion.20), channel_id=2, replica_groups=mesh['rep'=32,'tp'=16] {'tp'}, dimensions={0}, use_global_device_ids=true | all-gather | bytes 696320 | tf_op jit(solution)/shard_map/all_gather | solution.py:120
  220.5 0.3 reduce_sum.52
  220.8 0.2 fusion.19
  221.0 1.6 fusion.30
  (23 shorter events, 0.3 us)
Async XLA Ops:
  6.5 88.2 %copy-start = (bf16[44,1,8,256]{3,2,1,0:T(8,128)(2,1)S(1)}, bf16[44,1,8,256]{3,2,1,0:T(8,128)(2,1)}, u32[]{:S(2)}) copy-start(bf16[44,1,8,256]{3,2,1,0:T(8,128)(2,1)} %param.12) | copy-start | bytes 540676
  34.2 4.2 %copy-start.2 = (bf16[2,64,512]{2,1,0:T(8,128)(2,1)S(1)}, bf16[2,64,512]{2,1,0:T(8,128)(2,1)}, u32[]{:S(2)}) copy-start(bf16[2,64,512]{2,1,0:T(8,128)(2,1)} %param.16) | copy-start | bytes 393220
  34.2 53.6 %all-to-all-start.2 = ((bf16[32,2,64,256]{3,2,1,0:T(8,128)(2,1)}), bf16[32,2,64,256]{3,2,1,0:T(8,128)(2,1)S(1)}, u32[]{:S(2)}, u32[]{:S(2)}) async-start(bf16[32,2,64,256]{3,2,1,0:T(8,128)(2,1)} %copy.44), calls=%async_computation.3 | async-start | bytes 4194304 | tf_op jit(solution)/shard_map/all_to_all | solution.py:108
  44.0 50.2 %copy-start.3 = (s32[20,6]{0,1:T(8,128)S(1)}, s32[20,6]{0,1:T(8,128)}, u32[]{:S(2)}) copy-start(s32[20,6]{0,1:T(8,128)} %param.14) | copy-start | bytes 1444
  44.0 50.5 %copy-start.1 = (bf16[320,512]{1,0:T(8,128)(2,1)S(1)}, bf16[320,512]{1,0:T(8,128)(2,1)}, u32[]{:S(2)}) copy-start(bf16[320,512]{1,0:T(8,128)(2,1)} %param.10) | copy-start | bytes 983044
  44.0 51.4 %copy-start.4 = (s32[20]{0:T(128)S(1)}, s32[20]{0:T(128)}, u32[]{:S(2)}) copy-start(s32[20]{0:T(128)} %param.13) | copy-start | bytes 244
  44.0 51.5 %copy-start.5 = (bf16[320,256]{1,0:T(8,128)(2,1)S(1)}, bf16[320,256]{1,0:T(8,128)(2,1)}, u32[]{:S(2)}) copy-start(bf16[320,256]{1,0:T(8,128)(2,1)} %param.11) | copy-start | bytes 491524
  87.8 101.9 %all-to-all-start.1 = ((bf16[32,2,64,512]{3,2,1,0:T(8,128)(2,1)}), bf16[32,2,64,512]{3,2,1,0:T(8,128)(2,1)}, u32[]{:S(2)}, u32[]{:S(2)}) async-start(bf16[32,2,64,512]{3,2,1,0:T(8,128)(2,1)} %copy.40), calls=%async_computation.2 | async-start | bytes 8388608 | tf_op jit(solution)/shard_map/all_to_all | solution.py:107
  94.0 127.0 %reduce-scatter.2.cloned.1.call-start = ((), (), s32[]{:S(2)}) async-start(), calls=%async_computation.4 | async-start | bytes 2785280 | tf_op jit(solution)/shard_map/reduce_scatter | solution.py:69
Sparse Core Ops, SparseCore 0:
  104.6 65.6 reduce-scatter.1
